TPU v7x, 256 devices: a whole 4x4x8 slice. The times are simulated.
256 devices in a mesh: grid: 16 (over y_hi, z), states: 16 (over y_lo, x, core).
Axes of the slice: x: 4, y: 4 (y_hi: 2, y_lo: 2; y = y_hi * 2 + y_lo), z: 8, core: 2. Of those that a mesh axis runs over, the one named last changes fastest.
Arguments:
- states_in: float32 [16, 256, 32, 128], P('states', 'grid'), may hold values from -10 to 10
- potential: float32 [256, 32, 128], P('grid'), may hold values from -2 to 0.5
- projectors: bfloat16 [16, 32, 8, 4096], P('grid', 'states'), may hold values from -0.0625 to 0.0625
- proj_gains: bfloat16 [16, 32, 8], P('grid', 'states'), may hold values from 1 to 6
- atom_owner: int32 [160], P('grid'), may hold values from 0 to 15, as said below
- atom_rows: int32 [160, 32], P('grid'), may hold values from -1 to 8191, as said below
- wrap_rows: int32 [32], replicated, may hold values from 0 to 31, as said below
Outputs:
- filtered: float32 [16, 256, 32, 128], P('states', 'grid')
Inputs may be any that keep to these rules, and one draw needn't show every extreme that they name: `atom_owner`: atom a belongs to tile a // 10. At most 2 atoms of one tile share an owner, and one owner takes exactly 2 atoms of every tile. `atom_rows`: A row r is the line of cells at x = r // 32, y = r % 32. Each list holds distinct rows whose x lies in the atom's own tile of 16 planes, followed by -1 entries; each list has 16 rows or more, and the first atom of every tile fills all 32. wrap_rows[y] = (y + t) mod 32 for one t of 1 to 31.
All inputs are finite; a program needn't handle non-finite values.
Results may differ from a plain program's by a relative error of at most 0.00082.
Values may be sent and summed in bfloat16 or wider, within the bound.
No kernel may reach another device: no remote copies, remote signals or barrier semaphores. Data moves between devices by JAX's collectives and lax.ppermute only.
A program may use at most 64 MiB of HBM per device.

v0:
```python
import math
import jax
import jax.numpy as jnp
from jax import lax
from jax.sharding import PartitionSpec as P

RADIUS = 6
PAIR_CAP = 2
MIXED_WEIGHT = 0.7
CENTER = 12.0
HALF_WIDTH = 8.0


def padded_2(shard, sides, width):
    for axis, dim in sides:
        count, length = (lax.axis_size(axis), shard.shape[dim])
        up = [(i, (i + 1) % count) for i in range(count)]
        down = [(j, i) for i, j in up]
        last = lax.slice_in_dim(shard, length - width, length, axis=dim)
        initial = lax.slice_in_dim(shard, 0, width, axis=dim)
        before = lax.ppermute(last, axis, up)
        after = lax.ppermute(initial, axis, down)
        shard = jnp.concatenate([before, shard, after], axis=dim)
    return shard


def second_table(radius):
    weights = [-2.0 * sum((1.0 / (k * k) for k in range(1, radius + 1)))]
    for k in range(1, radius + 1):
        weights.append(
            2.0
            * (-1) ** (k + 1)
            * math.factorial(radius) ** 2
            / (k * k * math.factorial(radius - k) * math.factorial(radius + k))
        )
    return weights


def first_table(radius):
    weights = [0.0]
    for k in range(1, radius + 1):
        weights.append(
            (-1) ** (k + 1)
            * math.factorial(radius) ** 2
            / (k * math.factorial(radius - k) * math.factorial(radius + k))
        )
    return weights


def laplacian(padded, plane_count):
    second_weights = second_table(RADIUS)
    first_weights = first_table(RADIUS)
    interior = padded[:, RADIUS : RADIUS + plane_count]
    line_depth = interior.shape[3]
    z_padded = jnp.pad(interior, ((0, 0), (0, 0), (0, 0), (RADIUS, RADIUS)))
    summed = 3.0 * second_weights[0] * interior
    y_slope = jnp.zeros_like(padded)
    for k in range(1, RADIUS + 1):
        summed = summed + second_weights[k] * (
            padded[:, RADIUS + k : RADIUS + k + plane_count]
            + padded[:, RADIUS - k : RADIUS - k + plane_count]
        )
        summed = summed + second_weights[k] * (jnp.roll(interior, -k, 2) + jnp.roll(interior, k, 2))
        summed = summed + second_weights[k] * (
            z_padded[:, :, :, RADIUS + k : RADIUS + k + line_depth]
            + z_padded[:, :, :, RADIUS - k : RADIUS - k + line_depth]
        )
        y_slope = y_slope + first_weights[k] * (jnp.roll(padded, -k, 2) - jnp.roll(padded, k, 2))
    cross_term = jnp.zeros_like(interior)
    for k in range(1, RADIUS + 1):
        cross_term = cross_term + first_weights[k] * (
            y_slope[:, RADIUS + k : RADIUS + k + plane_count]
            - y_slope[:, RADIUS - k : RADIUS - k + plane_count]
        )
    return summed + MIXED_WEIGHT * cross_term


def shards(states_in, potential, projectors, proj_gains, atom_owner, atom_rows, wrap_rows):
    state_count, tile_width, breadth, line_depth = states_in.shape
    n_grid = lax.axis_size("grid")
    tile_index = lax.axis_index("grid")
    tile_lines = tile_width * breadth
    block_rows = atom_rows.shape[1]
    line_span = block_rows * line_depth
    proj_count = projectors.shape[2]
    home_count = atom_owner.shape[0]
    row_order = jnp.arange(breadth, dtype=jnp.int32)
    unwrap_rows = jnp.sum(
        row_order[None, :] * (wrap_rows[None, :] == row_order[:, None]).astype(jnp.int32), axis=1
    )
    atom_order = jnp.arange(home_count, dtype=jnp.int32)
    same_owner = (atom_owner[:, None] == atom_owner[None, :]) & (
        atom_order[None, :] < atom_order[:, None]
    )
    owner_rank = jnp.sum(same_owner.astype(jnp.int32), axis=1)
    atom_slot = atom_owner * PAIR_CAP + owner_rank
    local_rows = jnp.where(atom_rows >= 0, atom_rows - tile_index * tile_lines, tile_lines)
    full_proj, full_gain = (
        lax.all_gather(projectors, "states", axis=1, tiled=True),
        lax.all_gather(proj_gains, "states", axis=1, tiled=True),
    )
    full_proj = full_proj.reshape(n_grid, PAIR_CAP, proj_count, line_span)
    full_gain = full_gain.reshape(n_grid, PAIR_CAP, proj_count)

    def extended(grid_field):
        padded = padded_2(grid_field, (("grid", 1),), RADIUS)
        low_rim = padded[:, :RADIUS]
        high_rim = padded[:, RADIUS + tile_width :]
        low_rim = jnp.where(tile_index == 0, jnp.take(low_rim, wrap_rows, axis=2), low_rim)
        high_rim = jnp.where(
            tile_index == n_grid - 1, jnp.take(high_rim, unwrap_rows, axis=2), high_rim
        )
        return jnp.concatenate([low_rim, padded[:, RADIUS : RADIUS + tile_width], high_rim], axis=1)

    def pick_rows(grid_field):
        lines_here = grid_field.reshape(state_count, tile_lines, line_depth)
        picked = jnp.take(lines_here, local_rows, axis=1, mode="fill", fill_value=0.0).astype(
            jnp.bfloat16
        )
        return jnp.swapaxes(picked.reshape(state_count, home_count, line_span), 0, 1)

    def place_rows(projected):
        pieces = (
            jnp.swapaxes(projected, 0, 1)
            .reshape(state_count, home_count, block_rows, line_depth)
            .astype(jnp.float32)
        )
        summed = (
            jnp.zeros((state_count, tile_lines, line_depth), jnp.float32)
            .at[:, local_rows]
            .add(pieces, mode="drop")
        )
        return summed.reshape(state_count, tile_width, breadth, line_depth)

    def at_owner(received):
        coefficients = jnp.einsum(
            "gpjc,gpsc->gpsj", full_proj, received, preferred_element_type=jnp.float32
        )
        scaled = (coefficients * full_gain[:, :, None, :].astype(jnp.float32)).astype(jnp.bfloat16)
        projected = jnp.einsum(
            "gpjc,gpsj->gpsc", full_proj, scaled, preferred_element_type=jnp.float32
        ).astype(jnp.bfloat16)
        return lax.all_to_all(projected, "grid", split_axis=0, concat_axis=0, tiled=True)

    def nonlocal_part(grid_field):
        picked = pick_rows(grid_field)
        outbox = (
            jnp.zeros((n_grid * PAIR_CAP, state_count, line_span), jnp.bfloat16)
            .at[atom_slot]
            .set(picked)
        )
        outbox = outbox.reshape(n_grid, PAIR_CAP, state_count, line_span)
        returned_rows = at_owner(
            lax.all_to_all(outbox, "grid", split_axis=0, concat_axis=0, tiled=True)
        )
        projected = jnp.take(
            returned_rows.reshape(n_grid * PAIR_CAP, state_count, line_span), atom_slot, axis=0
        )
        return place_rows(projected)

    def operate(grid_field):
        padded = extended(grid_field)
        return (
            -0.5 * laplacian(padded, tile_width)
            + potential[None] * grid_field
            + nonlocal_part(grid_field)
        )

    def shifted(grid_field):
        return (operate(grid_field) - CENTER * grid_field) / HALF_WIDTH

    first_term = shifted(states_in)
    second_term = 2.0 * shifted(first_term) - states_in
    return 2.0 * shifted(second_term) - first_term


def solution(mesh):
    in_specs = (
        P("states", "grid", None, None),
        P("grid", None, None),
        P("grid", "states", None, None),
        P("grid", "states", None),
        P("grid"),
        P("grid", None),
        P(),
    )
    out_specs = P("states", "grid", None, None)
    return jax.shard_map(shards, mesh=mesh, in_specs=in_specs, out_specs=out_specs, check_vma=False)
```

profile of v0, /device:TPU:32, one launch (start us, length us, event | category | flops | bytes accessed | tf_op | source)
XLA Modules:
  0.0 244.3 jit_solution(14710537106557358727)
XLA Ops:
  11.1 2.1 gather_fusion.2
  15.9 13.5 %all-to-all-start = ((bf16[16,2,1,4096]{3,1,2,0:T(2,128)(2,1)}), bf16[16,2,1,4096]{3,1,2,0:T(2,128)(2,1)S(1)}, u32[]{:S(2)}, u32[]{:S(2)}) async-start(bf16[16,2,1,4096]{3,1,2,0:T(2,128)(2,1)} %reshape.2251), calls=%async_computation | async-start | bytes 524288 | tf_op jit(solution)/shard_map/all_to_all | solution.py:154
  36.3 18.8 %all_gather.7 = bf16[1,32,8]{2,0,1:T(2,128)(2,1)S(1)} all-gather(bf16[1,2,8]{2,0,1:T(2,128)(2,1)S(1)} %copy.162), channel_id=1, replica_groups=mesh['grid'=16,'states'=16] {'states'}, dimensions={1}, use_global_device_ids=true | all-gather | bytes 544 | tf_op jit(solution)/shard_map/all_gather | solution.py:100
  66.6 3.0 %all-gather.2.cloned.1.call-done = bf16[1,32,8,4096]{3,2,0,1:T(8,128)(2,1)} async-done(((bf16[1,2,8,4096]{3,2,0,1:T(8,128)(2,1)}), bf16[1,32,8,4096]{3,2,0,1:T(8,128)(2,1)}) %all-gather.2.cloned.1.call-update) | async-done | bytes 2097168 | tf_op jit(solution)/shard_map/all_gather | solution.py:99
  69.6 3.3 %fusion.46 = f32[16,2,1,8]{3,2,1,0:T(1,128)S(1)} fusion(bf16[16,2,8,4096]{3,2,1,0:T(8,128)(2,1)} %bitcast.158, bf16[16,2,4096,1]{2,1,0,3:T(2,128)(2,1)} %bitcast.182), kind=kOutput, calls=%fused_computation.193 | convolution fusion | flops 2097152 | bytes 2360320 | tf_op jit(solution)/shard_map/gpjc,gpsc->gpsj/dot_general | solution.py:136
  74.7 9.6 %all-to-all-start.1 = ((bf16[16,2,1,4096]{3,1,2,0:T(2,128)(2,1)}), bf16[16,2,1,4096]{3,1,2,0:T(2,128)(2,1)}, u32[]{:S(2)}, u32[]{:S(2)}) async-start(bf16[16,2,1,4096]{3,1,2,0:T(2,128)(2,1)} %bitcast.153), calls=%async_computation.1 | async-start | bytes 524288 | tf_op jit(solution)/shard_map/all_to_all | solution.py:143
  85.8 2.5 %fusion.25 = f32[1,28,32,128]{3,1,2,0:T(8,128)S(1)} fusion(f32[1,6,32,128]{3,1,2,0:T(8,128)S(1)} %fusion.285, f32[1,16,32,128]{3,1,2,0:T(8,128)S(1)} %copy.128, f32[1,6,32,128]{3,1,2,0:T(8,128)S(1)} %fusion.284, f32[1,28,31,128]{3,1,2,0:T(8,128)S(1)} %get-tuple-element.79, f32[1,28,31,128]{3,1,2,0:T(8,128)S(1)} %get-tuple-element.78, ...), kind=kLoop, calls=%fused_computation.148 | loop fusion | flops 3784704 | bytes 6393856 | tf_op jit(solution)/shard_map/add | solution.py:68
  88.2 8.2 %all-to-all-done.1 = bf16[16,2,1,4096]{3,1,2,0:T(2,128)(2,1)} async-done(((bf16[16,2,1,4096]{3,1,2,0:T(2,128)(2,1)}), bf16[16,2,1,4096]{3,1,2,0:T(2,128)(2,1)}, u32[]{:S(2)}, u32[]{:S(2)}) %all-to-all-start.1) | async-done | bytes 262176 | tf_op jit(solution)/shard_map/all_to_all | solution.py:143
  100.6 2.7 %scatter_custom_fusion.1 = f32[512,128]{1,0:T(8,128)} fusion(s32[320]{0:T(512)} %copy-done.43, f32[320,128]{1,0:T(8,128)} %reshape.2406, f32[]{:T(128)} %constant.58.clone.1), kind=kCustom, calls=%fused_computation.503 | custom fusion | flops 40960 | bytes 262656 | tf_op jit(solution)/shard_map/scatter-add | solution.py:131
  103.2 4.3 %broadcast_multiply_fusion = (f32[1,16,32,128]{3,1,2,0:T(8,128)S(1)}, f32[1,16,32,128]{3,1,2,0:T(8,128)}) fusion(f32[1,16,32,128]{3,1,2,0:T(8,128)S(1)} %copy.128, f32[1,16,32,128]{3,2,1,0:T(8,128)} %bitcast.168, f32[16,32,128]{2,1,0:T(8,128)S(1)} %copy-done.2, f32[1,28,32,128]{3,1,2,0:T(8,128)S(1)} %fusion.25, f32[1,16,26,128]{3,1,2,0:T(8,128)} %get-tuple-element.153, ...), kind=kLoop, calls=%fused_computation.505 | loop fusion | flops 6881280 | bytes 7798784 | tf_op jit(solution)/shard_map/div | solution.py:170
  121.9 7.9 %all-to-all-start.2 = ((bf16[16,2,1,4096]{3,1,2,0:T(2,128)(2,1)}), bf16[16,2,1,4096]{3,1,2,0:T(2,128)(2,1)}, u32[]{:S(2)}, u32[]{:S(2)}) async-start(bf16[16,2,1,4096]{3,1,2,0:T(2,128)(2,1)} %reshape.2257), calls=%async_computation.2 | async-start | bytes 524288 | tf_op jit(solution)/shard_map/all_to_all | solution.py:154
  138.2 2.3 all-to-all-done.2
  140.5 2.4 fusion.44
  144.7 7.3 %all-to-all-start.3 = ((bf16[16,2,1,4096]{3,1,2,0:T(2,128)(2,1)}), bf16[16,2,1,4096]{3,1,2,0:T(2,128)(2,1)}, u32[]{:S(2)}, u32[]{:S(2)}) async-start(bf16[16,2,1,4096]{3,1,2,0:T(2,128)(2,1)} %bitcast.155), calls=%async_computation.3 | async-start | bytes 524288 | tf_op jit(solution)/shard_map/all_to_all | solution.py:143
  153.5 2.5 %fusion.16 = f32[1,28,32,128]{3,1,2,0:T(8,128)S(1)} fusion(f32[1,6,32,128]{3,1,2,0:T(8,128)S(1)} %fusion.283, f32[1,16,32,128]{3,1,2,0:T(8,128)S(1)} %get-tuple-element.6, f32[1,6,32,128]{3,1,2,0:T(8,128)S(1)} %fusion.282, f32[1,28,31,128]{3,1,2,0:T(8,128)S(1)} %get-tuple-element.57, f32[1,28,31,128]{3,1,2,0:T(8,128)S(1)} %get-tuple-element.56, ...), kind=kLoop, calls=%fused_computation.135 | loop fusion | flops 3784704 | bytes 6393856 | tf_op jit(solution)/shard_map/add | solution.py:68
  156.0 6.7 %all-to-all-done.3 = bf16[16,2,1,4096]{3,1,2,0:T(2,128)(2,1)} async-done(((bf16[16,2,1,4096]{3,1,2,0:T(2,128)(2,1)}), bf16[16,2,1,4096]{3,1,2,0:T(2,128)(2,1)}, u32[]{:S(2)}, u32[]{:S(2)}) %all-to-all-start.3) | async-done | bytes 262176 | tf_op jit(solution)/shard_map/all_to_all | solution.py:143
  166.8 2.7 %scatter_custom_fusion.3 = f32[512,128]{1,0:T(8,128)} fusion(s32[320]{0:T(512)} %copy-done.43, f32[320,128]{1,0:T(8,128)} %reshape.2426, f32[]{:T(128)} %constant.58.clone.1), kind=kCustom, calls=%fused_computation.501 | custom fusion | flops 40960 | bytes 262656 | tf_op jit(solution)/shard_map/scatter-add | solution.py:131
  169.5 3.9 %fusion.111 = f32[1,16,32,128]{3,1,2,0:T(8,128)S(1)} fusion(f32[1,16,32,128]{3,1,2,0:T(8,128)S(1)} %get-tuple-element.6, f32[1,6,32,128]{3,1,2,0:T(8,128)} %copy-done.6, f32[1,6,32,128]{3,1,2,0:T(8,128)S(1)} %fusion.283, f32[1,28,32,128]{3,1,2,0:T(8,128)S(1)} %fusion.16, f32[1,16,1,128]{3,1,2,0:T(8,128)} %get-tuple-element.127, ...), kind=kLoop, calls=%fused_computation.258 | loop fusion | flops 6946816 | bytes 8060928 | tf_op jit(solution)/shard_map/sub | solution.py:173
  181.6 2.0 collective-permute-start.5
  187.7 7.6 %all-to-all-start.4 = ((bf16[16,2,1,4096]{3,1,2,0:T(2,128)(2,1)}), bf16[16,2,1,4096]{3,1,2,0:T(2,128)(2,1)S(1)}, u32[]{:S(2)}, u32[]{:S(2)}) async-start(bf16[16,2,1,4096]{3,1,2,0:T(2,128)(2,1)} %reshape.2262), calls=%async_computation.4 | async-start | bytes 524288 | tf_op jit(solution)/shard_map/all_to_all | solution.py:154
  209.5 9.6 %all-to-all-start.5 = ((bf16[16,2,1,4096]{3,1,2,0:T(2,128)(2,1)}), bf16[16,2,1,4096]{3,1,2,0:T(2,128)(2,1)S(1)}, u32[]{:S(2)}, u32[]{:S(2)}) async-start(bf16[16,2,1,4096]{3,1,2,0:T(2,128)(2,1)} %bitcast.157), calls=%async_computation.5 | async-start | bytes 524288 | tf_op jit(solution)/shard_map/all_to_all | solution.py:143
  219.3 3.0 %fusion.7 = f32[1,28,32,128]{3,1,2,0:T(8,128)S(1)} fusion(f32[1,6,32,128]{3,1,2,0:T(8,128)S(1)} %fusion.281, f32[1,16,32,128]{3,1,2,0:T(8,128)S(1)} %fusion.111, f32[1,6,32,128]{3,1,2,0:T(8,128)S(1)} %fusion.280, f32[1,28,31,128]{3,1,2,0:T(8,128)S(1)} %get-tuple-element.35, f32[1,28,31,128]{3,1,2,0:T(8,128)S(1)} %get-tuple-element.34, ...), kind=kLoop, calls=%fused_computation.122 | loop fusion | flops 3784704 | bytes 6393856 | tf_op jit(solution)/shard_map/add | solution.py:68
  222.4 7.2 %all-to-all-done.5 = bf16[16,2,1,4096]{3,1,2,0:T(2,128)(2,1)S(1)} async-done(((bf16[16,2,1,4096]{3,1,2,0:T(2,128)(2,1)}), bf16[16,2,1,4096]{3,1,2,0:T(2,128)(2,1)S(1)}, u32[]{:S(2)}, u32[]{:S(2)}) %all-to-all-start.5) | async-done | bytes 262176 | tf_op jit(solution)/shard_map/all_to_all | solution.py:143
  233.2 3.4 %fusion.66 = f32[1,16,32,128]{3,1,2,0:T(8,128)S(1)} fusion(f32[1,16,32,128]{3,1,2,0:T(8,128)S(1)} %fusion.111, f32[1,6,32,128]{3,1,2,0:T(8,128)S(1)} %fusion.280, f32[1,6,32,128]{3,1,2,0:T(8,128)S(1)} %fusion.281, f32[1,28,32,128]{3,1,2,0:T(8,128)S(1)} %fusion.7, f32[1,16,1,128]{3,1,2,0:T(8,128)} %get-tuple-element.101, ...), kind=kLoop, calls=%fused_computation.213 | loop fusion | flops 7012352 | bytes 7798784 | tf_op jit(solution)/shard_map/sub | solution.py:174
  (269 shorter events, 93.3 us)
Async XLA Ops:
  6.5 23.6 %copy-start.52 = (s32[32]{0:T(128)S(1)}, s32[32]{0:T(128)}, u32[]{:S(2)}) copy-start(s32[32]{0:T(128)} %param.19) | copy-start | bytes 388
  7.7 50.7 %collective-permute-start = (f32[1,6,32,128]{3,1,2,0:T(8,128)S(1)}, f32[1,6,32,128]{3,1,2,0:T(8,128)S(1)}, u32[]{:S(2)}, u32[]{:S(2)}) collective-permute-start(f32[1,6,32,128]{3,1,2,0:T(8,128)S(1)} %get-tuple-element.157), channel_id=1, source_target_pairs={{16,0},{32,16},{48,32},{64,48},{80,64},{96,80},{112,96},{128,112},... | collective-permute-start | bytes 294920 | tf_op jit(solution)/shard_map/ppermute | solution.py:22
  9.6 49.4 %collective-permute-start.1 = (f32[1,6,32,128]{3,1,2,0:T(8,128)S(1)}, f32[1,6,32,128]{3,1,2,0:T(8,128)S(1)}, u32[]{:S(2)}, u32[]{:S(2)}) collective-permute-start(f32[1,6,32,128]{3,1,2,0:T(8,128)S(1)} %get-tuple-element.156), channel_id=1, source_target_pairs={{0,16},{16,32},{32,48},{48,64},{64,80},{80,96},{96,112},{112,128},... | collective-permute-start | bytes 294920 | tf_op jit(solution)/shard_map/ppermute | solution.py:21
  13.4 22.9 %copy-start.53 = (bf16[1,2,8]{2,1,0:T(2,128)(2,1)S(1)}, bf16[1,2,8]{2,1,0:T(2,128)(2,1)}, u32[]{:S(2)}) copy-start(bf16[1,2,8]{2,1,0:T(2,128)(2,1)} %param.16) | copy-start | bytes 100
  14.2 41.7 %copy-start.50 = (s32[10]{0:T(128)}, s32[10]{0:T(128)S(1)}, u32[]{:S(2)}) copy-start(s32[10]{0:T(128)S(1)} %get-tuple-element.11) | copy-start | bytes 124
  15.9 50.8 %all-to-all-start = ((bf16[16,2,1,4096]{3,1,2,0:T(2,128)(2,1)}), bf16[16,2,1,4096]{3,1,2,0:T(2,128)(2,1)S(1)}, u32[]{:S(2)}, u32[]{:S(2)}) async-start(bf16[16,2,1,4096]{3,1,2,0:T(2,128)(2,1)} %reshape.2251), calls=%async_computation | async-start | bytes 524288 | tf_op jit(solution)/shard_map/all_to_all | solution.py:154
  29.4 40.2 %all-gather.2.cloned.1.call-start = ((), (), s32[]{:S(2)}) async-start(), calls=%async_computation.6 | async-start | bytes 2228224 | tf_op jit(solution)/shard_map/all_gather | solution.py:99
  30.2 29.4 %copy-start.48 = (pred[32]{0:T(512)(128)(4,1)}, pred[32]{0:T(512)(128)(4,1)S(1)}, u32[]{:S(2)}) copy-start(pred[32]{0:T(512)(128)(4,1)S(1)} %compare_and_fusion.3) | copy-start | bytes 100
  30.3 29.5 %copy-start.46 = (pred[32]{0:T(512)(128)(4,1)}, pred[32]{0:T(512)(128)(4,1)S(1)}, u32[]{:S(2)}) copy-start(pred[32]{0:T(512)(128)(4,1)S(1)} %compare_and_fusion.2) | copy-start | bytes 100
  36.2 22.8 %copy-start.44 = (s32[1024]{0:T(1024)}, s32[1024]{0:T(1024)S(1)}, u32[]{:S(2)}) copy-start(s32[1024]{0:T(1024)S(1)} %pad_clamp_fusion.3) | copy-start | bytes 12292
  59.9 24.6 %copy-start.5 = (f32[1,6,32,128]{3,1,2,0:T(8,128)}, f32[1,6,32,128]{3,1,2,0:T(8,128)S(1)}, u32[]{:S(2)}) copy-start(f32[1,6,32,128]{3,1,2,0:T(8,128)S(1)} %fusion.284) | copy-start | bytes 294916
  74.7 21.7 %all-to-all-start.1 = ((bf16[16,2,1,4096]{3,1,2,0:T(2,128)(2,1)}), bf16[16,2,1,4096]{3,1,2,0:T(2,128)(2,1)}, u32[]{:S(2)}, u32[]{:S(2)}) async-start(bf16[16,2,1,4096]{3,1,2,0:T(2,128)(2,1)} %bitcast.153), calls=%async_computation.1 | async-start | bytes 524288 | tf_op jit(solution)/shard_map/all_to_all | solution.py:143
  88.2 15.0 %copy-start.2 = (f32[16,32,128]{2,1,0:T(8,128)S(1)}, f32[16,32,128]{2,1,0:T(8,128)}, u32[]{:S(2)}) copy-start(f32[16,32,128]{2,1,0:T(8,128)} %param.14) | copy-start | bytes 786436
  112.7 18.6 %copy-start.49 = (pred[32]{0:T(512)(128)(4,1)S(1)}, pred[32]{0:T(512)(128)(4,1)}, u32[]{:S(2)}) copy-start(pred[32]{0:T(512)(128)(4,1)} %copy-done.48) | copy-start | bytes 100
  112.7 18.7 %copy-start.47 = (pred[32]{0:T(512)(128)(4,1)S(1)}, pred[32]{0:T(512)(128)(4,1)}, u32[]{:S(2)}) copy-start(pred[32]{0:T(512)(128)(4,1)} %copy-done.46) | copy-start | bytes 100
  115.8 14.0 %collective-permute-start.2 = (f32[1,6,32,128]{3,1,2,0:T(8,128)S(1)}, f32[1,6,32,128]{3,1,2,0:T(8,128)S(1)}, u32[]{:S(2)}, u32[]{:S(2)}) collective-permute-start(f32[1,6,32,128]{3,1,2,0:T(8,128)S(1)} %get-tuple-element.130), channel_id=1, source_target_pairs={{16,0},{32,16},{48,32},{64,48},{80,64},{96,80},{112,96},{128,112},... | collective-permute-start | bytes 294920 | tf_op jit(solution)/shard_map/ppermute | solution.py:22
  115.9 14.6 %collective-permute-start.3 = (f32[1,6,32,128]{3,1,2,0:T(8,128)S(1)}, f32[1,6,32,128]{3,1,2,0:T(8,128)S(1)}, u32[]{:S(2)}, u32[]{:S(2)}) collective-permute-start(f32[1,6,32,128]{3,1,2,0:T(8,128)S(1)} %get-tuple-element.131), channel_id=1, source_target_pairs={{0,16},{16,32},{32,48},{48,64},{64,80},{80,96},{96,112},{112,128},... | collective-permute-start | bytes 294920 | tf_op jit(solution)/shard_map/ppermute | solution.py:21
  121.9 18.6 %all-to-all-start.2 = ((bf16[16,2,1,4096]{3,1,2,0:T(2,128)(2,1)}), bf16[16,2,1,4096]{3,1,2,0:T(2,128)(2,1)}, u32[]{:S(2)}, u32[]{:S(2)}) async-start(bf16[16,2,1,4096]{3,1,2,0:T(2,128)(2,1)} %reshape.2257), calls=%async_computation.2 | async-start | bytes 524288 | tf_op jit(solution)/shard_map/all_to_all | solution.py:154
  131.5 20.7 %copy-start.6 = (f32[1,6,32,128]{3,1,2,0:T(8,128)}, f32[1,6,32,128]{3,1,2,0:T(8,128)S(1)}, u32[]{:S(2)}) copy-start(f32[1,6,32,128]{3,1,2,0:T(8,128)S(1)} %fusion.282) | copy-start | bytes 294916
  144.7 18.0 %all-to-all-start.3 = ((bf16[16,2,1,4096]{3,1,2,0:T(2,128)(2,1)}), bf16[16,2,1,4096]{3,1,2,0:T(2,128)(2,1)}, u32[]{:S(2)}, u32[]{:S(2)}) async-start(bf16[16,2,1,4096]{3,1,2,0:T(2,128)(2,1)} %bitcast.155), calls=%async_computation.3 | async-start | bytes 524288 | tf_op jit(solution)/shard_map/all_to_all | solution.py:143
  181.6 13.7 %collective-permute-start.4 = (f32[1,6,32,128]{3,1,2,0:T(8,128)S(1)}, f32[1,6,32,128]{3,1,2,0:T(8,128)S(1)}, u32[]{:S(2)}, u32[]{:S(2)}) collective-permute-start(f32[1,6,32,128]{3,1,2,0:T(8,128)S(1)} %get-tuple-element.104), channel_id=1, source_target_pairs={{16,0},{32,16},{48,32},{64,48},{80,64},{96,80},{112,96},{128,112},... | collective-permute-start | bytes 294920 | tf_op jit(solution)/shard_map/ppermute | solution.py:22
  181.6 14.4 %collective-permute-start.5 = (f32[1,6,32,128]{3,1,2,0:T(8,128)S(1)}, f32[1,6,32,128]{3,1,2,0:T(8,128)S(1)}, u32[]{:S(2)}, u32[]{:S(2)}) collective-permute-start(f32[1,6,32,128]{3,1,2,0:T(8,128)S(1)} %get-tuple-element.105), channel_id=1, source_target_pairs={{0,16},{16,32},{32,48},{48,64},{64,80},{80,96},{96,112},{112,128},... | collective-permute-start | bytes 294920 | tf_op jit(solution)/shard_map/ppermute | solution.py:21
  187.7 18.5 %all-to-all-start.4 = ((bf16[16,2,1,4096]{3,1,2,0:T(2,128)(2,1)}), bf16[16,2,1,4096]{3,1,2,0:T(2,128)(2,1)S(1)}, u32[]{:S(2)}, u32[]{:S(2)}) async-start(bf16[16,2,1,4096]{3,1,2,0:T(2,128)(2,1)} %reshape.2262), calls=%async_computation.4 | async-start | bytes 524288 | tf_op jit(solution)/shard_map/all_to_all | solution.py:154
  209.5 20.2 %all-to-all-start.5 = ((bf16[16,2,1,4096]{3,1,2,0:T(2,128)(2,1)}), bf16[16,2,1,4096]{3,1,2,0:T(2,128)(2,1)S(1)}, u32[]{:S(2)}, u32[]{:S(2)}) async-start(bf16[16,2,1,4096]{3,1,2,0:T(2,128)(2,1)} %bitcast.157), calls=%async_computation.5 | async-start | bytes 524288 | tf_op jit(solution)/shard_map/all_to_all | solution.py:143
  (43 other events, 251.7 us)
Sparse Core Ops, SparseCore 0:
  32.0 37.4 all-gather.1
where the time goes:
time: 245 us; the launch traced here: 244 us
  local copies, waits for them, and re-layouts  77.8 us (32%)
  starting transfers between devices  61.8 us (25%)
  other arithmetic  34.1 us (14%)
  waiting for transfers between devices  28.1 us (11%)
  blocking collectives  18.8 us (8%)
  between operations  14.5 us (6%)
  matrix products  9.17 us (4%)
    all_to_all x3, starting transfers between devices, nonlocal_part(): lax.all_to_all(outbox, 'grid', split_axis=0, concat_axis=0, tiled=True)  29.1 us
    all_to_all x3, starting transfers between devices, at_owner(): lax.all_to_all(projected, 'grid', split_axis=0, concat_axis=0, tiled=True)  26.5 us
    all_to_all x3, waiting for transfers between devices, at_owner(): lax.all_to_all(projected, 'grid', split_axis=0, concat_axis=0, tiled=True)  22.1 us
    slice x33, local copies, waits for them, and re-layouts, laplacian(): jnp.roll(padded, k, 2)  21.4 us
    all_gather x1, blocking collectives, shards(): lax.all_gather(proj_gains, 'states', axis=1, tiled=True)  18.8 us
    slice x24, local copies, waits for them, and re-layouts, laplacian(): jnp.roll(interior, k, 2)  17.4 us
    slice x12, local copies, waits for them, and re-layouts, laplacian(): jnp.roll(interior, -k, 2) + jnp.roll(interior, k, 2)  8.69 us
    add x3, other arithmetic, laplacian(): y_slope + first_weights[k] * (jnp.roll(padded, -k, 2) - jnp.roll(padded,...  7.96 us
  transfers between devices with their start and end apart: 13, of which 5 were waited for; matrix products, arithmetic and copies ran while one was open for 24% of the time, Pallas kernels for 0%

commit v1 on v0

--- a/solution.py
+++ b/solution.py
@@ -1,14 +1,27 @@
+import functools
 import math
 import jax
 import jax.numpy as jnp
 from jax import lax
 from jax.sharding import PartitionSpec as P
+from jax.lax import all_to_all, axis_size
 
 RADIUS = 6
 PAIR_CAP = 2
 MIXED_WEIGHT = 0.7
 CENTER = 12.0
 HALF_WIDTH = 8.0
+
+
+def _answer_scenes(payload, chip_axis, dimension_no):
+    tall = axis_size(chip_axis)
+    x_now = jnp.stack(tall * [payload], 0)
+    b_now = all_to_all(x_now, chip_axis, 0, 0)
+    seen_now = jnp.concatenate(b_now, dimension_no)
+    return seen_now
+
+
+cover_knots = functools.partial(_answer_scenes, chip_axis="states", dimension_no=1)
 
 
 def padded_2(shard, sides, width):
@@ -97,7 +110,7 @@
     local_rows = jnp.where(atom_rows >= 0, atom_rows - tile_index * tile_lines, tile_lines)
     full_proj, full_gain = (
         lax.all_gather(projectors, "states", axis=1, tiled=True),
-        lax.all_gather(proj_gains, "states", axis=1, tiled=True),
+        cover_knots(proj_gains),
     )
     full_proj = full_proj.reshape(n_grid, PAIR_CAP, proj_count, line_span)
     full_gain = full_gain.reshape(n_grid, PAIR_CAP, proj_count)

time: 245 us -> 244 us (level)
  blocking collectives: 18.8 us -> 0 us
  waiting for transfers between devices: 28.1 us -> 42.7 us
  starting transfers between devices: 61.8 us -> 65.5 us
    all_gather x1 -> x0, blocking collectives: 18.8 us -> none  [shards(): lax.all_gather(proj_gains, 'states', axis=1, tiled=True)]
    all_gather x1, waiting for transfers between devices: 2.95 us -> 16.7 us  [shards(): lax.all_gather(projectors, 'states', axis=1, tiled=True)]
    all_to_all x0 -> x1, starting transfers between devices: none -> 4.52 us  [_answer_scenes(): b_now = all_to_all(x_now, chip_axis, 0, 0)]
  transfers between devices with their start and end apart: 13 -> 14, of which waited for: 5 -> 6; matrix products, arithmetic and copies ran while one was open for 24% -> 25% of each run, Pallas kernels for 0% -> 0%
where the time goes in v1:
time: 244 us; the launch traced here: 243 us
  local copies, waits for them, and re-layouts  77.9 us (32%)
  starting transfers between devices  65.5 us (27%)
  waiting for transfers between devices  42.7 us (18%)
  other arithmetic  32.8 us (13%)
  between operations  14.5 us (6%)
  matrix products  9.17 us (4%)
    all_to_all x3, starting transfers between devices, nonlocal_part(): lax.all_to_all(outbox, 'grid', split_axis=0, concat_axis=0, tiled=True)  29.1 us
    all_to_all x3, starting transfers between devices, at_owner(): lax.all_to_all(projected, 'grid', split_axis=0, concat_axis=0, tiled=True)  25.8 us
    all_to_all x3, waiting for transfers between devices, at_owner(): lax.all_to_all(projected, 'grid', split_axis=0, concat_axis=0, tiled=True)  22.1 us
    slice x33, local copies, waits for them, and re-layouts, laplacian(): jnp.roll(padded, k, 2)  21.4 us
    slice x24, local copies, waits for them, and re-layouts, laplacian(): jnp.roll(interior, k, 2)  17.4 us
    all_gather x1, waiting for transfers between devices, shards(): lax.all_gather(projectors, 'states', axis=1, tiled=True)  16.7 us
    slice x12, local copies, waits for them, and re-layouts, laplacian(): jnp.roll(interior, -k, 2) + jnp.roll(interior, k, 2)  8.69 us
    add x3, other arithmetic, laplacian(): y_slope + first_weights[k] * (jnp.roll(padded, -k, 2) - jnp.roll(padded,...  7.96 us
  transfers between devices with their start and end apart: 14, of which 6 were waited for; matrix products, arithmetic and copies ran while one was open for 25% of the time, Pallas kernels for 0%

profile of v1, /device:TPU:32, one launch (start us, length us, event | category | flops | bytes accessed | tf_op | source)
XLA Modules:
  0.0 242.6 jit_solution(5326627559402964139)
XLA Ops:
  10.6 2.1 gather_fusion.2
  15.3 13.5 %all-to-all-start = ((bf16[16,2,1,4096]{3,1,2,0:T(2,128)(2,1)}), bf16[16,2,1,4096]{3,1,2,0:T(2,128)(2,1)S(1)}, u32[]{:S(2)}, u32[]{:S(2)}) async-start(bf16[16,2,1,4096]{3,1,2,0:T(2,128)(2,1)} %reshape.2254), calls=%async_computation | async-start | bytes 524288 | tf_op jit(solution)/shard_map/all_to_all | solution.py:167
  47.8 4.5 %all-to-all-start.1 = ((bf16[16,1,2,8]{3,2,1,0:T(2,128)(2,1)}), bf16[16,1,2,8]{3,2,1,0:T(2,128)(2,1)S(1)}, u32[]{:S(2)}, u32[]{:S(2)}) async-start(bf16[16,1,2,8]{3,2,1,0:T(2,128)(2,1)} %stack.2), calls=%async_computation.1 | async-start | bytes 16384 | tf_op jit(solution)/shard_map/all_to_all | solution.py:19
  52.4 16.7 %all-gather.2.cloned.1.call-done = bf16[1,32,8,4096]{3,2,0,1:T(8,128)(2,1)} async-done(((bf16[1,2,8,4096]{3,2,0,1:T(8,128)(2,1)}), bf16[1,32,8,4096]{3,2,0,1:T(8,128)(2,1)}) %all-gather.2.cloned.1.call-update) | async-done | bytes 2097168 | tf_op jit(solution)/shard_map/all_gather | solution.py:112
  69.0 3.3 %fusion.46 = f32[16,2,1,8]{3,2,1,0:T(1,128)S(1)} fusion(bf16[16,2,8,4096]{3,2,1,0:T(8,128)(2,1)} %bitcast.163, bf16[16,2,4096,1]{2,1,0,3:T(2,128)(2,1)} %bitcast.187), kind=kOutput, calls=%fused_computation.193 | convolution fusion | flops 2097152 | bytes 2360320 | tf_op jit(solution)/shard_map/gpjc,gpsc->gpsj/dot_general | solution.py:149
  74.2 9.7 %all-to-all-start.2 = ((bf16[16,2,1,4096]{3,1,2,0:T(2,128)(2,1)}), bf16[16,2,1,4096]{3,1,2,0:T(2,128)(2,1)}, u32[]{:S(2)}, u32[]{:S(2)}) async-start(bf16[16,2,1,4096]{3,1,2,0:T(2,128)(2,1)} %bitcast.158), calls=%async_computation.2 | async-start | bytes 524288 | tf_op jit(solution)/shard_map/all_to_all | solution.py:156
  85.4 2.5 %fusion.25 = f32[1,28,32,128]{3,1,2,0:T(8,128)S(1)} fusion(f32[1,6,32,128]{3,1,2,0:T(8,128)S(1)} %fusion.285, f32[1,16,32,128]{3,1,2,0:T(8,128)S(1)} %copy.127, f32[1,6,32,128]{3,1,2,0:T(8,128)S(1)} %fusion.284, f32[1,28,31,128]{3,1,2,0:T(8,128)S(1)} %get-tuple-element.79, f32[1,28,31,128]{3,1,2,0:T(8,128)S(1)} %get-tuple-element.78, ...), kind=kLoop, calls=%fused_computation.148 | loop fusion | flops 3784704 | bytes 6393856 | tf_op jit(solution)/shard_map/add | solution.py:81
  87.9 8.2 %all-to-all-done.2 = bf16[16,2,1,4096]{3,1,2,0:T(2,128)(2,1)} async-done(((bf16[16,2,1,4096]{3,1,2,0:T(2,128)(2,1)}), bf16[16,2,1,4096]{3,1,2,0:T(2,128)(2,1)}, u32[]{:S(2)}, u32[]{:S(2)}) %all-to-all-start.2) | async-done | bytes 262176 | tf_op jit(solution)/shard_map/all_to_all | solution.py:156
  100.2 2.7 %scatter_custom_fusion.1 = f32[512,128]{1,0:T(8,128)} fusion(s32[320]{0:T(512)} %copy-done.39, f32[320,128]{1,0:T(8,128)} %reshape.2409, f32[]{:T(128)} %constant.58.clone.1), kind=kCustom, calls=%fused_computation.503 | custom fusion | flops 40960 | bytes 262656 | tf_op jit(solution)/shard_map/scatter-add | solution.py:144
  102.9 4.3 %broadcast_multiply_fusion = (f32[1,16,32,128]{3,1,2,0:T(8,128)S(1)}, f32[1,16,32,128]{3,1,2,0:T(8,128)}) fusion(f32[1,16,32,128]{3,1,2,0:T(8,128)S(1)} %copy.127, f32[1,16,32,128]{3,2,1,0:T(8,128)} %bitcast.173, f32[16,32,128]{2,1,0:T(8,128)S(1)} %copy-done.2, f32[1,28,32,128]{3,1,2,0:T(8,128)S(1)} %fusion.25, f32[1,16,26,128]{3,1,2,0:T(8,128)} %get-tuple-element.153, ...), kind=kLoop, calls=%fused_computation.505 | loop fusion | flops 6881280 | bytes 7798784 | tf_op jit(solution)/shard_map/div | solution.py:183
  121.5 7.9 %all-to-all-start.3 = ((bf16[16,2,1,4096]{3,1,2,0:T(2,128)(2,1)}), bf16[16,2,1,4096]{3,1,2,0:T(2,128)(2,1)}, u32[]{:S(2)}, u32[]{:S(2)}) async-start(bf16[16,2,1,4096]{3,1,2,0:T(2,128)(2,1)} %reshape.2260), calls=%async_computation.3 | async-start | bytes 524288 | tf_op jit(solution)/shard_map/all_to_all | solution.py:167
  137.8 2.3 all-to-all-done.3
  140.1 2.4 fusion.44
  144.3 7.3 %all-to-all-start.4 = ((bf16[16,2,1,4096]{3,1,2,0:T(2,128)(2,1)}), bf16[16,2,1,4096]{3,1,2,0:T(2,128)(2,1)}, u32[]{:S(2)}, u32[]{:S(2)}) async-start(bf16[16,2,1,4096]{3,1,2,0:T(2,128)(2,1)} %bitcast.160), calls=%async_computation.4 | async-start | bytes 524288 | tf_op jit(solution)/shard_map/all_to_all | solution.py:156
  153.1 2.5 %fusion.16 = f32[1,28,32,128]{3,1,2,0:T(8,128)S(1)} fusion(f32[1,6,32,128]{3,1,2,0:T(8,128)S(1)} %fusion.283, f32[1,16,32,128]{3,1,2,0:T(8,128)S(1)} %get-tuple-element.6, f32[1,6,32,128]{3,1,2,0:T(8,128)S(1)} %fusion.282, f32[1,28,31,128]{3,1,2,0:T(8,128)S(1)} %get-tuple-element.57, f32[1,28,31,128]{3,1,2,0:T(8,128)S(1)} %get-tuple-element.56, ...), kind=kLoop, calls=%fused_computation.135 | loop fusion | flops 3784704 | bytes 6393856 | tf_op jit(solution)/shard_map/add | solution.py:81
  155.6 6.7 %all-to-all-done.4 = bf16[16,2,1,4096]{3,1,2,0:T(2,128)(2,1)} async-done(((bf16[16,2,1,4096]{3,1,2,0:T(2,128)(2,1)}), bf16[16,2,1,4096]{3,1,2,0:T(2,128)(2,1)}, u32[]{:S(2)}, u32[]{:S(2)}) %all-to-all-start.4) | async-done | bytes 262176 | tf_op jit(solution)/shard_map/all_to_all | solution.py:156
  166.4 2.7 %scatter_custom_fusion.3 = f32[512,128]{1,0:T(8,128)} fusion(s32[320]{0:T(512)} %copy-done.39, f32[320,128]{1,0:T(8,128)} %reshape.2429, f32[]{:T(128)} %constant.58.clone.1), kind=kCustom, calls=%fused_computation.501 | custom fusion | flops 40960 | bytes 262656 | tf_op jit(solution)/shard_map/scatter-add | solution.py:144
  169.1 3.9 %fusion.111 = f32[1,16,32,128]{3,1,2,0:T(8,128)S(1)} fusion(f32[1,16,32,128]{3,1,2,0:T(8,128)S(1)} %get-tuple-element.6, f32[1,6,32,128]{3,1,2,0:T(8,128)} %copy-done.6, f32[1,6,32,128]{3,1,2,0:T(8,128)S(1)} %fusion.283, f32[1,28,32,128]{3,1,2,0:T(8,128)S(1)} %fusion.16, f32[1,16,1,128]{3,1,2,0:T(8,128)} %get-tuple-element.127, ...), kind=kLoop, calls=%fused_computation.258 | loop fusion | flops 6946816 | bytes 8060928 | tf_op jit(solution)/shard_map/sub | solution.py:186
  181.2 2.0 collective-permute-start.5
  187.3 7.6 %all-to-all-start.5 = ((bf16[16,2,1,4096]{3,1,2,0:T(2,128)(2,1)}), bf16[16,2,1,4096]{3,1,2,0:T(2,128)(2,1)S(1)}, u32[]{:S(2)}, u32[]{:S(2)}) async-start(bf16[16,2,1,4096]{3,1,2,0:T(2,128)(2,1)} %reshape.2265), calls=%async_computation.5 | async-start | bytes 524288 | tf_op jit(solution)/shard_map/all_to_all | solution.py:167
  208.8 8.7 %all-to-all-start.6 = ((bf16[16,2,1,4096]{3,1,2,0:T(2,128)(2,1)}), bf16[16,2,1,4096]{3,1,2,0:T(2,128)(2,1)S(1)}, u32[]{:S(2)}, u32[]{:S(2)}) async-start(bf16[16,2,1,4096]{3,1,2,0:T(2,128)(2,1)} %bitcast.162), calls=%async_computation.6 | async-start | bytes 524288 | tf_op jit(solution)/shard_map/all_to_all | solution.py:156
  217.6 3.0 %fusion.7 = f32[1,28,32,128]{3,1,2,0:T(8,128)S(1)} fusion(f32[1,6,32,128]{3,1,2,0:T(8,128)S(1)} %fusion.281, f32[1,16,32,128]{3,1,2,0:T(8,128)S(1)} %fusion.111, f32[1,6,32,128]{3,1,2,0:T(8,128)S(1)} %fusion.280, f32[1,28,31,128]{3,1,2,0:T(8,128)S(1)} %get-tuple-element.35, f32[1,28,31,128]{3,1,2,0:T(8,128)S(1)} %get-tuple-element.34, ...), kind=kLoop, calls=%fused_computation.122 | loop fusion | flops 3784704 | bytes 6393856 | tf_op jit(solution)/shard_map/add | solution.py:81
  220.8 7.3 %all-to-all-done.6 = bf16[16,2,1,4096]{3,1,2,0:T(2,128)(2,1)S(1)} async-done(((bf16[16,2,1,4096]{3,1,2,0:T(2,128)(2,1)}), bf16[16,2,1,4096]{3,1,2,0:T(2,128)(2,1)S(1)}, u32[]{:S(2)}, u32[]{:S(2)}) %all-to-all-start.6) | async-done | bytes 262176 | tf_op jit(solution)/shard_map/all_to_all | solution.py:156
  231.5 3.4 %fusion.66 = f32[1,16,32,128]{3,1,2,0:T(8,128)S(1)} fusion(f32[1,16,32,128]{3,1,2,0:T(8,128)S(1)} %fusion.111, f32[1,6,32,128]{3,1,2,0:T(8,128)S(1)} %fusion.280, f32[1,6,32,128]{3,1,2,0:T(8,128)S(1)} %fusion.281, f32[1,28,32,128]{3,1,2,0:T(8,128)S(1)} %fusion.7, f32[1,16,1,128]{3,1,2,0:T(8,128)} %get-tuple-element.101, ...), kind=kLoop, calls=%fused_computation.213 | loop fusion | flops 7012352 | bytes 7798784 | tf_op jit(solution)/shard_map/sub | solution.py:187
  (265 shorter events, 93.0 us)
Async XLA Ops:
  6.5 23.0 %copy-start.51 = (s32[32]{0:T(128)S(1)}, s32[32]{0:T(128)}, u32[]{:S(2)}) copy-start(s32[32]{0:T(128)} %param.19) | copy-start | bytes 388
  7.7 31.3 %collective-permute-start = (f32[1,6,32,128]{3,1,2,0:T(8,128)S(1)}, f32[1,6,32,128]{3,1,2,0:T(8,128)S(1)}, u32[]{:S(2)}, u32[]{:S(2)}) collective-permute-start(f32[1,6,32,128]{3,1,2,0:T(8,128)S(1)} %get-tuple-element.157), channel_id=1, source_target_pairs={{16,0},{32,16},{48,32},{64,48},{80,64},{96,80},{112,96},{128,112},... | collective-permute-start | bytes 294920 | tf_op jit(solution)/shard_map/ppermute | solution.py:35
  9.6 30.0 %collective-permute-start.1 = (f32[1,6,32,128]{3,1,2,0:T(8,128)S(1)}, f32[1,6,32,128]{3,1,2,0:T(8,128)S(1)}, u32[]{:S(2)}, u32[]{:S(2)}) collective-permute-start(f32[1,6,32,128]{3,1,2,0:T(8,128)S(1)} %get-tuple-element.156), channel_id=1, source_target_pairs={{0,16},{16,32},{32,48},{48,64},{64,80},{80,96},{96,112},{112,128},... | collective-permute-start | bytes 294920 | tf_op jit(solution)/shard_map/ppermute | solution.py:34
  10.6 21.3 %copy-start.39 = (s32[320]{0:T(512)}, s32[320]{0:T(512)S(1)}, u32[]{:S(2)}) copy-start(s32[320]{0:T(512)S(1)} %reshape.2407) | copy-start | bytes 3844
  13.6 22.9 %copy-start.48 = (s32[10]{0:T(128)}, s32[10]{0:T(128)S(1)}, u32[]{:S(2)}) copy-start(s32[10]{0:T(128)S(1)} %get-tuple-element.11) | copy-start | bytes 124
  15.3 31.9 %all-to-all-start = ((bf16[16,2,1,4096]{3,1,2,0:T(2,128)(2,1)}), bf16[16,2,1,4096]{3,1,2,0:T(2,128)(2,1)S(1)}, u32[]{:S(2)}, u32[]{:S(2)}) async-start(bf16[16,2,1,4096]{3,1,2,0:T(2,128)(2,1)} %reshape.2254), calls=%async_computation | async-start | bytes 524288 | tf_op jit(solution)/shard_map/all_to_all | solution.py:167
  28.8 40.3 %all-gather.2.cloned.1.call-start = ((), (), s32[]{:S(2)}) async-start(), calls=%async_computation.7 | async-start | bytes 2228224 | tf_op jit(solution)/shard_map/all_gather | solution.py:112
  40.5 43.6 %copy-start.5 = (f32[1,6,32,128]{3,1,2,0:T(8,128)}, f32[1,6,32,128]{3,1,2,0:T(8,128)S(1)}, u32[]{:S(2)}) copy-start(f32[1,6,32,128]{3,1,2,0:T(8,128)S(1)} %fusion.284) | copy-start | bytes 294916
  47.2 21.9 %copy-start.25 = (bf16[16,2,1,4096]{3,1,2,0:T(2,128)(2,1)}, bf16[16,2,1,4096]{3,1,2,0:T(2,128)(2,1)S(1)}, u32[]{:S(2)}) copy-start(bf16[16,2,1,4096]{3,1,2,0:T(2,128)(2,1)S(1)} %all-to-all-done) | copy-start | bytes 786436
  47.8 24.5 %all-to-all-start.1 = ((bf16[16,1,2,8]{3,2,1,0:T(2,128)(2,1)}), bf16[16,1,2,8]{3,2,1,0:T(2,128)(2,1)S(1)}, u32[]{:S(2)}, u32[]{:S(2)}) async-start(bf16[16,1,2,8]{3,2,1,0:T(2,128)(2,1)} %stack.2), calls=%async_computation.1 | async-start | bytes 16384 | tf_op jit(solution)/shard_map/all_to_all | solution.py:19
  72.3 70.2 %copy-start.34 = (bf16[16,1,2,8]{3,2,1,0:T(2,128)(2,1)}, bf16[16,1,2,8]{3,2,1,0:T(2,128)(2,1)S(1)}, u32[]{:S(2)}) copy-start(bf16[16,1,2,8]{3,2,1,0:T(2,128)(2,1)S(1)} %all-to-all-done.1) | copy-start | bytes 1540
  74.2 21.9 %all-to-all-start.2 = ((bf16[16,2,1,4096]{3,1,2,0:T(2,128)(2,1)}), bf16[16,2,1,4096]{3,1,2,0:T(2,128)(2,1)}, u32[]{:S(2)}, u32[]{:S(2)}) async-start(bf16[16,2,1,4096]{3,1,2,0:T(2,128)(2,1)} %bitcast.158), calls=%async_computation.2 | async-start | bytes 524288 | tf_op jit(solution)/shard_map/all_to_all | solution.py:156
  112.3 18.6 %copy-start.46 = (pred[32]{0:T(512)(128)(4,1)S(1)}, pred[32]{0:T(512)(128)(4,1)}, u32[]{:S(2)}) copy-start(pred[32]{0:T(512)(128)(4,1)} %copy-done.45) | copy-start | bytes 100
  112.3 18.7 %copy-start.43 = (pred[32]{0:T(512)(128)(4,1)S(1)}, pred[32]{0:T(512)(128)(4,1)}, u32[]{:S(2)}) copy-start(pred[32]{0:T(512)(128)(4,1)} %copy-done.42) | copy-start | bytes 100
  115.4 14.0 %collective-permute-start.2 = (f32[1,6,32,128]{3,1,2,0:T(8,128)S(1)}, f32[1,6,32,128]{3,1,2,0:T(8,128)S(1)}, u32[]{:S(2)}, u32[]{:S(2)}) collective-permute-start(f32[1,6,32,128]{3,1,2,0:T(8,128)S(1)} %get-tuple-element.130), channel_id=1, source_target_pairs={{16,0},{32,16},{48,32},{64,48},{80,64},{96,80},{112,96},{128,112},... | collective-permute-start | bytes 294920 | tf_op jit(solution)/shard_map/ppermute | solution.py:35
  115.5 14.6 %collective-permute-start.3 = (f32[1,6,32,128]{3,1,2,0:T(8,128)S(1)}, f32[1,6,32,128]{3,1,2,0:T(8,128)S(1)}, u32[]{:S(2)}, u32[]{:S(2)}) collective-permute-start(f32[1,6,32,128]{3,1,2,0:T(8,128)S(1)} %get-tuple-element.131), channel_id=1, source_target_pairs={{0,16},{16,32},{32,48},{48,64},{64,80},{80,96},{96,112},{112,128},... | collective-permute-start | bytes 294920 | tf_op jit(solution)/shard_map/ppermute | solution.py:34
  121.5 18.6 %all-to-all-start.3 = ((bf16[16,2,1,4096]{3,1,2,0:T(2,128)(2,1)}), bf16[16,2,1,4096]{3,1,2,0:T(2,128)(2,1)}, u32[]{:S(2)}, u32[]{:S(2)}) async-start(bf16[16,2,1,4096]{3,1,2,0:T(2,128)(2,1)} %reshape.2260), calls=%async_computation.3 | async-start | bytes 524288 | tf_op jit(solution)/shard_map/all_to_all | solution.py:167
  131.1 20.7 %copy-start.6 = (f32[1,6,32,128]{3,1,2,0:T(8,128)}, f32[1,6,32,128]{3,1,2,0:T(8,128)S(1)}, u32[]{:S(2)}) copy-start(f32[1,6,32,128]{3,1,2,0:T(8,128)S(1)} %fusion.282) | copy-start | bytes 294916
  144.3 18.0 %all-to-all-start.4 = ((bf16[16,2,1,4096]{3,1,2,0:T(2,128)(2,1)}), bf16[16,2,1,4096]{3,1,2,0:T(2,128)(2,1)}, u32[]{:S(2)}, u32[]{:S(2)}) async-start(bf16[16,2,1,4096]{3,1,2,0:T(2,128)(2,1)} %bitcast.160), calls=%async_computation.4 | async-start | bytes 524288 | tf_op jit(solution)/shard_map/all_to_all | solution.py:156
  178.1 18.4 %copy-start.44 = (pred[32]{0:T(512)(128)(4,1)S(1)}, pred[32]{0:T(512)(128)(4,1)}, u32[]{:S(2)}) copy-start(pred[32]{0:T(512)(128)(4,1)} %copy-done.42) | copy-start | bytes 100
  181.2 13.7 %collective-permute-start.4 = (f32[1,6,32,128]{3,1,2,0:T(8,128)S(1)}, f32[1,6,32,128]{3,1,2,0:T(8,128)S(1)}, u32[]{:S(2)}, u32[]{:S(2)}) collective-permute-start(f32[1,6,32,128]{3,1,2,0:T(8,128)S(1)} %get-tuple-element.104), channel_id=1, source_target_pairs={{16,0},{32,16},{48,32},{64,48},{80,64},{96,80},{112,96},{128,112},... | collective-permute-start | bytes 294920 | tf_op jit(solution)/shard_map/ppermute | solution.py:35
  181.2 14.4 %collective-permute-start.5 = (f32[1,6,32,128]{3,1,2,0:T(8,128)S(1)}, f32[1,6,32,128]{3,1,2,0:T(8,128)S(1)}, u32[]{:S(2)}, u32[]{:S(2)}) collective-permute-start(f32[1,6,32,128]{3,1,2,0:T(8,128)S(1)} %get-tuple-element.105), channel_id=1, source_target_pairs={{0,16},{16,32},{32,48},{48,64},{64,80},{80,96},{96,112},{112,128},... | collective-permute-start | bytes 294920 | tf_op jit(solution)/shard_map/ppermute | solution.py:34
  187.3 18.2 %all-to-all-start.5 = ((bf16[16,2,1,4096]{3,1,2,0:T(2,128)(2,1)}), bf16[16,2,1,4096]{3,1,2,0:T(2,128)(2,1)S(1)}, u32[]{:S(2)}, u32[]{:S(2)}) async-start(bf16[16,2,1,4096]{3,1,2,0:T(2,128)(2,1)} %reshape.2265), calls=%async_computation.5 | async-start | bytes 524288 | tf_op jit(solution)/shard_map/all_to_all | solution.py:167
  208.8 19.2 %all-to-all-start.6 = ((bf16[16,2,1,4096]{3,1,2,0:T(2,128)(2,1)}), bf16[16,2,1,4096]{3,1,2,0:T(2,128)(2,1)S(1)}, u32[]{:S(2)}, u32[]{:S(2)}) async-start(bf16[16,2,1,4096]{3,1,2,0:T(2,128)(2,1)} %bitcast.162), calls=%async_computation.6 | async-start | bytes 524288 | tf_op jit(solution)/shard_map/all_to_all | solution.py:156
  (42 other events, 273.6 us)
Sparse Core Ops, SparseCore 0:
  31.4 37.5 all-gather.1
